TPU v7x, 32 devices: a whole 2x2x4 slice. The times are simulated.
32 devices in a mesh: grp: 2 (over y), dp: 4 (over x, core), sp: 4 (over z).
Axes of the slice: x: 2, y: 2, z: 4, core: 2. Of those that a mesh axis runs over, the one named last changes fastest.
Arguments:
- rollout_rows: bfloat16 [4096, 5120], P(('grp', 'dp', 'sp')), parts along dimension 0, may hold values from -28 to 28
- routing: int32 [4096], P('grp'), parts along dimension 0, may hold values from 0 to 3, as said below
- segment_labels: int32 [8, 512], P(('grp', 'dp'), 'sp'), parts along dimension 0, may hold values from 0 to 3, never falling along the last dimension, each value on 1 to 256 neighbouring positions
- upstream: bfloat16 [8, 512, 4096], P(('grp', 'dp'), 'sp'), parts along dimension 0, may hold values from -24 to 24
- passes: int32 [32], P('grp'), parts along dimension 0, may hold values from 0 to 10
- group_ids: int32 [32], P('grp'), parts along dimension 0, may hold values from 0 to 1, as said below
Outputs:
- query_gradient: bfloat16 [8, 512, 4096], P(('grp', 'dp'), 'sp'), parts along dimension 0
- kv_grads: bfloat16 [8, 512, 1024], P(('grp', 'dp'), 'sp'), parts along dimension 0
There are 2 independent parts, one for each index of `grp`. A program takes and returns all parts, laid end to end along the dimension named above; each array names one. Nothing has to cross between parts.
Inputs may be any that keep to these rules, and one draw needn't show every extreme that they name: `routing`: among the rows of one column j (rows i with (i // 128) % (4) == j) every owner receives exactly 128 rows; the rows of one device go to each owner in numbers 0, 32 or 64, and every device sends exactly 64 rows to one owner. `group_ids`: every group holds exactly 8 completions.
All inputs are finite; a program needn't handle non-finite values.
Results may differ from a plain program's by a relative error of at most 0.012.
Values may be sent and summed in bfloat16 or wider, within the bound.
No kernel may reach another device: no remote copies, remote signals or barrier semaphores. Data moves between devices by JAX's collectives and lax.ppermute only.
A program may use at most 128 MiB of HBM per device.

v0:
```python
import math
import jax
import jax.numpy as jnp
import numpy as np
from jax import lax
from jax.sharding import PartitionSpec as P

QUERY_HEADS = 32
KEY_VALUE_HEADS = 4
HEAD_SIZE = 128
SEGS = 4
GROUP = 8
TESTS = 10


def slot_layout(row_list, sequence_split_size):
    token_rows = row_list.shape[0]
    per_dev = QUERY_HEADS // sequence_split_size
    query_group = QUERY_HEADS // KEY_VALUE_HEADS
    query_rows = row_list[:, : QUERY_HEADS * HEAD_SIZE].reshape(
        token_rows, sequence_split_size, per_dev * HEAD_SIZE
    )
    key_value_couples = row_list[:, QUERY_HEADS * HEAD_SIZE :].reshape(
        token_rows, 2, KEY_VALUE_HEADS, HEAD_SIZE
    )
    head_table = np.arange(sequence_split_size) * per_dev // query_group
    picked = jnp.transpose(key_value_couples[:, :, head_table, :], (0, 2, 1, 3)).reshape(
        token_rows, sequence_split_size, 2 * HEAD_SIZE
    )
    return jnp.concatenate([query_rows, picked], axis=2)


def group_advantage(passes, group_ids):
    reward = passes.astype(jnp.float32) / TESTS
    labels = jnp.arange(group_ids.shape[0] // GROUP, dtype=jnp.int32)
    member = (group_ids[:, None] == labels[None, :]).astype(jnp.float32)
    group_mean = jnp.sum(member * reward[:, None], axis=0) / jnp.sum(member, axis=0)
    return reward - jnp.sum(member * group_mean[None, :], axis=1)


def body(rollout_rows, routing, segment_labels, upstream, passes, group_ids):
    dp_size = lax.axis_size("dp")
    sequence_split_size = lax.axis_size("sp")
    dp_index = lax.axis_index("dp")
    sp_index = lax.axis_index("sp")
    token_rows = rollout_rows.shape[0]
    row_width = rollout_rows.shape[1]
    capacity = 2 * token_rows // dp_size
    per_dev = QUERY_HEADS // sequence_split_size
    seq_len = sequence_split_size * token_rows
    layout_plan = routing.reshape(dp_size, sequence_split_size, token_rows)
    column_plan = lax.dynamic_index_in_dim(layout_plan, sp_index, axis=1, keepdims=False)
    own_plan = lax.dynamic_index_in_dim(column_plan, dp_index, axis=0, keepdims=False)
    targets = jnp.arange(dp_size, dtype=jnp.int32)
    hit_table = (own_plan[:, None] == targets[None, :]).astype(jnp.int32)
    rank_rows = jnp.sum((jnp.cumsum(hit_table, axis=0) - 1) * hit_table, axis=1)
    slot_ids = own_plan * capacity + rank_rows
    positions = jnp.arange(token_rows, dtype=jnp.int32)
    outgoing = (
        jnp.zeros((dp_size * capacity, row_width), rollout_rows.dtype)
        .at[slot_ids]
        .set(rollout_rows)
    )
    arrived = lax.all_to_all(
        outgoing.reshape(dp_size, capacity, row_width),
        "dp",
        split_axis=0,
        concat_axis=0,
        tiled=True,
    )
    load_table = jnp.sum((column_plan == dp_index).astype(jnp.int32), axis=1)
    end_marks = jnp.cumsum(load_table)
    start_marks = end_marks - load_table
    source = jnp.sum((positions[:, None] >= end_marks[None, :]).astype(jnp.int32), axis=1)
    chosen_start = jnp.sum(
        jnp.where(source[:, None] == targets[None, :], start_marks[None, :], 0), axis=1
    )
    packed_tensor = arrived.reshape(dp_size * capacity, row_width)[
        source * capacity + positions - chosen_start
    ]
    regrouped = lax.all_to_all(
        slot_layout(packed_tensor, sequence_split_size),
        "sp",
        split_axis=1,
        concat_axis=0,
        tiled=True,
    )
    local_rows = regrouped.reshape(seq_len, regrouped.shape[2])
    full_seg = lax.all_gather(segment_labels, "sp", axis=1, tiled=True)[0]
    advantage = group_advantage(passes, group_ids)
    bin_adv = lax.dynamic_slice_in_dim(advantage, dp_index * SEGS, SEGS)
    own_seg = segment_labels[0]
    tok_adv = jnp.sum(
        jnp.where(
            own_seg[:, None] == jnp.arange(SEGS, dtype=jnp.int32)[None, :], bin_adv[None, :], 0.0
        ),
        axis=1,
    )
    weighted_result = (upstream[0].astype(jnp.float32) * tok_adv[:, None]).astype(jnp.bfloat16)
    grads_in = lax.all_to_all(
        weighted_result.reshape(token_rows, sequence_split_size, per_dev * HEAD_SIZE),
        "sp",
        split_axis=1,
        concat_axis=0,
        tiled=True,
    )
    grads_in = grads_in.reshape(seq_len, per_dev, HEAD_SIZE)
    query_rows = local_rows[:, : per_dev * HEAD_SIZE].reshape(seq_len, per_dev, HEAD_SIZE)
    key_matrix = local_rows[:, per_dev * HEAD_SIZE : (per_dev + 1) * HEAD_SIZE]
    value_matrix = local_rows[:, (per_dev + 1) * HEAD_SIZE :]
    block_rows = 512
    inv_root = 1.0 / math.sqrt(HEAD_SIZE)
    key_pos = jnp.arange(seq_len, dtype=jnp.int32)
    key_total = jnp.zeros((seq_len, HEAD_SIZE), jnp.float32)
    value_total = jnp.zeros((seq_len, HEAD_SIZE), jnp.float32)
    query_parts = []
    for block_start in range(0, seq_len, block_rows):
        block_end = block_start + block_rows
        query_block = query_rows[block_start:block_end]
        grad_block = grads_in[block_start:block_end]
        key_part = key_matrix[:block_end]
        value_part = value_matrix[:block_end]
        scores = (
            jnp.einsum("bhd,kd->hbk", query_block, key_part, preferred_element_type=jnp.float32)
            * inv_root
        )
        allowed = (full_seg[block_start:block_end, None] == full_seg[None, :block_end]) & (
            key_pos[None, :block_end] <= key_pos[block_start:block_end, None]
        )
        scores = jnp.where(allowed[None], scores, -1e30)
        row_top = jnp.max(scores, axis=2, keepdims=True)
        scaled_exp = jnp.exp(scores - row_top)
        weights = scaled_exp / jnp.sum(scaled_exp, axis=2, keepdims=True)
        weight_grads = jnp.einsum(
            "bhd,kd->hbk", grad_block, value_part, preferred_element_type=jnp.float32
        )
        row_dot = jnp.sum(weights * weight_grads, axis=2, keepdims=True)
        score_grads = (weights * (weight_grads - row_dot) * inv_root).astype(jnp.bfloat16)
        query_parts.append(
            jnp.einsum(
                "hbk,kd->bhd", score_grads, key_part, preferred_element_type=jnp.float32
            ).astype(jnp.bfloat16)
        )
        key_total = key_total.at[:block_end].add(
            jnp.einsum("hbk,bhd->kd", score_grads, query_block, preferred_element_type=jnp.float32)
        )
        value_total = value_total.at[:block_end].add(
            jnp.einsum(
                "hbk,bhd->kd",
                weights.astype(jnp.bfloat16),
                grad_block,
                preferred_element_type=jnp.float32,
            )
        )
    query_back = jnp.concatenate(query_parts, axis=0).reshape(
        sequence_split_size, token_rows, per_dev * HEAD_SIZE
    )
    query_gradient = lax.all_to_all(query_back, "sp", split_axis=0, concat_axis=2, tiled=True)
    partial_value = jnp.concatenate([key_total, value_total], axis=1).reshape(
        sequence_split_size, token_rows, 2 * HEAD_SIZE
    )
    key_value_pieces = lax.all_to_all(
        partial_value.astype(jnp.bfloat16), "sp", split_axis=0, concat_axis=0, tiled=True
    ).astype(partial_value.dtype)
    summed_total = jnp.sum(
        key_value_pieces.reshape(
            KEY_VALUE_HEADS, sequence_split_size // KEY_VALUE_HEADS, token_rows, 2, HEAD_SIZE
        ),
        axis=1,
    )
    kv_grads = (
        jnp.transpose(summed_total, (1, 2, 0, 3))
        .reshape(1, token_rows, 2 * KEY_VALUE_HEADS * HEAD_SIZE)
        .astype(jnp.bfloat16)
    )
    return (query_gradient, kv_grads)


def solution(mesh):
    return jax.shard_map(
        body,
        mesh=mesh,
        in_specs=(
            P(("grp", "dp", "sp"), None),
            P("grp"),
            P(("grp", "dp"), "sp"),
            P(("grp", "dp"), "sp", None),
            P("grp"),
            P("grp"),
        ),
        out_specs=(P(("grp", "dp"), "sp", None), P(("grp", "dp"), "sp", None)),
        check_vma=False,
    )
```

profile of v0, /device:TPU:0, one launch (start us, length us, event | category | flops | bytes accessed | tf_op | source)
XLA Modules:
  0.0 174.7 jit_solution(5603575321468290316)
XLA Ops:
  0.7 0.7 fusion.36
  1.5 0.2 reduce_window_sum.18
  1.6 0.2 select_reduce_fusion.1
  1.8 0.7 fusion.32
  2.5 5.0 %scatter_custom_fusion = bf16[256,5120]{1,0:T(8,128)(2,1)} fusion(s32[128]{0:T(128)S(1)} %fusion.32, bf16[128,5120]{1,0:T(8,128)(2,1)} %param.16, bf16[]{:T(256)} %constant.129.clone.1), kind=kCustom, calls=%fused_computation.24 | custom fusion | bytes 2621952 | tf_op jit(solution)/shard_map/scatter | solution.py:62
  7.5 4.2 %all-to-all-start = ((bf16[4,64,5120]{2,1,0:T(8,128)(2,1)}), bf16[4,64,5120]{2,1,0:T(8,128)(2,1)S(1)}, u32[]{:S(2)}, u32[]{:S(2)}) async-start(bf16[4,64,5120]{2,1,0:T(8,128)(2,1)} %bitcast.131), calls=%async_computation | async-start | bytes 5242880 | tf_op jit(solution)/shard_map/all_to_all | solution.py:64
  11.8 3.7 %reshape.279 = f32[128,4,1024]{2,1,0:T(4,128)} reshape(bf16[1,128,4096]{2,1,0:T(8,128)(2,1)} %param.19) | data formatting | bytes 3145728 | tf_op jit(solution)/shard_map/convert_element_type | solution.py:99
  15.5 0.1 convert_reduce_fusion.1
  15.6 0.1 select_reduce_fusion.3
  15.9 3.7 %fusion.11 = bf16[128,4,1024]{2,0,1:T(8,128)(2,1)} fusion(f32[128,4,1024]{2,1,0:T(4,128)} %reshape.279, f32[128]{0:T(128)S(1)} %select_reduce_fusion.2), kind=kLoop, calls=%fused_computation.20 | loop fusion | flops 1048576 | bytes 3146240 | tf_op jit(solution)/shard_map/convert_element_type | solution.py:99
  19.6 23.5 %all-to-all-done = bf16[4,64,5120]{2,1,0:T(8,128)(2,1)S(1)} async-done(((bf16[4,64,5120]{2,1,0:T(8,128)(2,1)}), bf16[4,64,5120]{2,1,0:T(8,128)(2,1)S(1)}, u32[]{:S(2)}, u32[]{:S(2)}) %all-to-all-start) | async-done | bytes 2621472 | tf_op jit(solution)/shard_map/all_to_all | solution.py:64
  43.1 5.7 %all-to-all-start.2 = ((bf16[128,4,1024]{2,0,1:T(8,128)(2,1)}), bf16[128,4,1024]{2,0,1:T(8,128)(2,1)}, u32[]{:S(2)}, u32[]{:S(2)}) async-start(bf16[128,4,1024]{2,0,1:T(8,128)(2,1)} %fusion.11), calls=%async_computation.2 | async-start | bytes 2097152 | tf_op jit(solution)/shard_map/all_to_all | solution.py:100
  48.8 0.9 fusion.31
  49.6 0.2 reduce-window.7
  49.8 0.1 convert_reduce_fusion
  49.9 0.2 select_reduce_fusion
  50.1 2.4 %gather_fusion = bf16[128,5120]{1,0:T(8,128)(2,1)} fusion(bf16[256,5120]{1,0:T(8,128)(2,1)S(1)} %bitcast.129, s32[1024]{0:T(1024)S(1)} %pad_clamp_fusion.1), kind=kCustom, calls=%fused_computation | custom fusion | bytes 2621952 | tf_op jit(solution)/shard_map/gather | solution.py:78
  52.5 1.0 slice.53
  53.5 1.3 slice.52
  54.9 0.2 reshape.273
  55.1 0.6 gather_fusion.1
  55.7 0.2 copy.61
  55.9 0.1 copy.63
  56.0 1.2 pad_maximum_fusion
  57.2 17.1 %all-to-all-done.2 = bf16[128,4,1024]{2,0,1:T(8,128)(2,1)} async-done(((bf16[128,4,1024]{2,0,1:T(8,128)(2,1)}), bf16[128,4,1024]{2,0,1:T(8,128)(2,1)}, u32[]{:S(2)}, u32[]{:S(2)}) %all-to-all-start.2) | async-done | bytes 1048608 | tf_op jit(solution)/shard_map/all_to_all | solution.py:100
  74.3 3.5 %all-to-all-start.1 = ((bf16[128,4,1280]{2,0,1:T(8,128)(2,1)}), bf16[128,4,1280]{2,0,1:T(8,128)(2,1)S(1)}, u32[]{:S(2)}, u32[]{:S(2)}) async-start(bf16[128,4,1280]{2,0,1:T(8,128)(2,1)} %pad_maximum_fusion), calls=%async_computation.1 | async-start | bytes 2621440 | tf_op jit(solution)/shard_map/all_to_all | solution.py:81
  77.9 26.7 %all_gather.3 = s32[1,512]{1,0:T(1,128)S(1)} all-gather(s32[1,128]{1,0:T(1,128)S(1)} %copy-done.3), channel_id=1, replica_groups=mesh['grp'=2,'dp'=4,'sp'=4] {'sp'}, dimensions={1}, use_global_device_ids=true | all-gather | bytes 2560 | tf_op jit(solution)/shard_map/all_gather | solution.py:89
  104.6 0.2 fusion.30
  104.8 2.6 %copy.83 = bf16[64,8,8,128]{3,2,1,0:T(8,128)(2,1)} copy(bf16[64,8,8,128]{3,1,2,0:T(8,128)(2,1)} %bitcast.57) | data formatting | bytes 2097152
  107.4 1.4 all-to-all-done.1
  108.8 1.1 slice.55
  109.9 1.5 copy.64
  111.4 1.5 fusion.4
  112.9 1.7 fusion.6
  114.7 3.0 %fusion = (f32[8,512]{1,0:T(8,128)S(1)}, f32[512,512,8]{1,0,2:T(8,128)S(1)}) fusion(f32[8,512]{1,0:T(8,128)S(1)} %fusion.6, f32[8,512]{1,0:T(8,128)S(1)} %get-tuple-element.52, f32[512,512,8]{1,0,2:T(8,128)S(1)} %get-tuple-element.53, pred[512,512]{0,1:T(8,128)(4,1)S(1)} %get-tuple-element.51, bf16[512,8,128]{2,1,0:T(8,128)(2,1)S(1)} %bitcast.141, ...), kind=kOutput, calls=%fused_computation.5 | convolution fusion | flops 549449728 | bytes 18268160 | tf_op jit(solution)/shard_map/bhd,kd->hbk/dot_general | solution.py:134
  117.7 4.6 %multiply_convert_fusion = (bf16[512,512,8]{1,0,2:T(8,128)(2,1)}, bf16[512,512,8]{1,0,2:T(8,128)(2,1)S(1)}) fusion(f32[512,512,8]{1,0,2:T(8,128)S(1)} %get-tuple-element.55, f32[512,8]{0,1:T(8,128)S(1)} %bitcast.150, f32[512,8]{0,1:T(8,128)S(1)} %bitcast.148, f32[512,8]{0,1:T(8,128)S(1)} %bitcast.147, f32[512,512,8]{1,0,2:T(8,128)S(1)} %get-tuple-element.53, ...), kind=kLoop, calls=%fused_computation.10 | loop fusion | flops 18874368 | bytes 25477120 | tf_op jit(solution)/shard_map/convert_element_type | solution.py:138
  122.3 3.6 %fusion.22 = bf16[4,128,128]{1,2,0:T(8,128)(2,1)S(1)} fusion(bf16[4,128,512,8]{2,1,0,3:T(8,128)(2,1)} %bitcast.143, bf16[512,8,128,1]{0,2,3,1:T(8,128)(2,1)S(1)} %bitcast.137), kind=kOutput, calls=%fused_computation.29 | convolution fusion | flops 536936448 | bytes 5373952 | tf_op jit(solution)/shard_map/hbk,bhd->kd/dot_general | solution.py:145
  125.9 1.5 fusion.23
  127.5 0.7 pad_maximum_fusion.1
  128.2 7.7 %all-to-all-start.4 = ((bf16[4,128,256]{1,2,0:T(8,128)(2,1)}), bf16[4,128,256]{1,2,0:T(8,128)(2,1)S(1)}, u32[]{:S(2)}, u32[]{:S(2)}) async-start(bf16[4,128,256]{1,2,0:T(8,128)(2,1)} %pad_maximum_fusion.1), calls=%async_computation.4 | async-start | bytes 524288 | tf_op jit(solution)/shard_map/all_to_all | solution.py:162
  135.8 7.8 %fusion.15 = bf16[512,8,128]{0,2,1:T(8,128)(2,1)S(1)} fusion(f32[512,512,8]{1,0,2:T(8,128)} %copy-done.1, f32[8,512]{1,0:T(8,128)S(1)} %get-tuple-element.54, f32[512,512,8]{1,0,2:T(8,128)} %copy-done, f32[8,512]{1,0:T(8,128)S(1)} %fusion.6, f32[8,512]{1,0:T(8,128)S(1)} %get-tuple-element.52, pred[512,512]{0,1:T(8,128)(4,1)S(1)} %get-tuple-element.51, ...), kind=kOutput, calls=%fused_computation.22 | convolution fusion | flops 554172416 | bytes 18268160 | tf_op jit(solution)/shard_map/hbk,kd->bhd/dot_general | solution.py:140
  143.6 0.3 reshape.278
  143.9 1.1 copy.70
  145.1 5.1 %all-to-all-start.3 = ((bf16[4,128,1024]{1,2,0:T(8,128)(2,1)}), bf16[4,128,1024]{1,2,0:T(8,128)(2,1)S(1)}, u32[]{:S(2)}, u32[]{:S(2)}) async-start(bf16[4,128,1024]{1,2,0:T(8,128)(2,1)} %copy.70), calls=%async_computation.3 | async-start | bytes 2097152 | tf_op jit(solution)/shard_map/all_to_all | solution.py:158
  150.1 0.2 copy.72
  150.3 0.9 convert_element_type.78
  151.2 22.2 %all-to-all-done.3 = bf16[4,128,1024]{1,2,0:T(8,128)(2,1)S(1)} async-done(((bf16[4,128,1024]{1,2,0:T(8,128)(2,1)}), bf16[4,128,1024]{1,2,0:T(8,128)(2,1)S(1)}, u32[]{:S(2)}, u32[]{:S(2)}) %all-to-all-start.3) | async-done | bytes 1048608 | tf_op jit(solution)/shard_map/all_to_all | solution.py:158
  173.4 1.3 copy.73
  (26 shorter events, 0.4 us)
Async XLA Ops:
  0.6 14.8 %copy-start.5 = (s32[16]{0:T(128)S(1)}, s32[16]{0:T(128)}, u32[]{:S(2)}) copy-start(s32[16]{0:T(128)} %param.20) | copy-start | bytes 196
  0.6 14.8 %copy-start.4 = (s32[16]{0:T(128)S(1)}, s32[16]{0:T(128)}, u32[]{:S(2)}) copy-start(s32[16]{0:T(128)} %param.21) | copy-start | bytes 196
  0.7 15.1 %copy-start.3 = (s32[1,128]{1,0:T(1,128)S(1)}, s32[1,128]{1,0:T(1,128)}, u32[]{:S(2)}) copy-start(s32[1,128]{1,0:T(1,128)} %param.18) | copy-start | bytes 1540
  7.5 35.6 %all-to-all-start = ((bf16[4,64,5120]{2,1,0:T(8,128)(2,1)}), bf16[4,64,5120]{2,1,0:T(8,128)(2,1)S(1)}, u32[]{:S(2)}, u32[]{:S(2)}) async-start(bf16[4,64,5120]{2,1,0:T(8,128)(2,1)} %bitcast.131), calls=%async_computation | async-start | bytes 5242880 | tf_op jit(solution)/shard_map/all_to_all | solution.py:64
  43.1 31.2 %all-to-all-start.2 = ((bf16[128,4,1024]{2,0,1:T(8,128)(2,1)}), bf16[128,4,1024]{2,0,1:T(8,128)(2,1)}, u32[]{:S(2)}, u32[]{:S(2)}) async-start(bf16[128,4,1024]{2,0,1:T(8,128)(2,1)} %fusion.11), calls=%async_computation.2 | async-start | bytes 2097152 | tf_op jit(solution)/shard_map/all_to_all | solution.py:100
  74.3 34.4 %all-to-all-start.1 = ((bf16[128,4,1280]{2,0,1:T(8,128)(2,1)}), bf16[128,4,1280]{2,0,1:T(8,128)(2,1)S(1)}, u32[]{:S(2)}, u32[]{:S(2)}) async-start(bf16[128,4,1280]{2,0,1:T(8,128)(2,1)} %pad_maximum_fusion), calls=%async_computation.1 | async-start | bytes 2621440 | tf_op jit(solution)/shard_map/all_to_all | solution.py:81
  111.4 3.3 %copy-start.2 = (bf16[64,8,8,128]{3,2,1,0:T(8,128)(2,1)S(1)}, bf16[64,8,8,128]{3,2,1,0:T(8,128)(2,1)}, u32[]{:S(2)}) copy-start(bf16[64,8,8,128]{3,2,1,0:T(8,128)(2,1)} %copy.83) | copy-start | bytes 3145732
  112.9 4.8 %copy-start = (f32[512,512,8]{1,0,2:T(8,128)}, f32[512,512,8]{1,0,2:T(8,128)S(1)}, u32[]{:S(2)}) copy-start(f32[512,512,8]{1,0,2:T(8,128)S(1)} %get-tuple-element.53) | copy-start | bytes 25165828
  117.7 4.6 %copy-start.1 = (f32[512,512,8]{1,0,2:T(8,128)}, f32[512,512,8]{1,0,2:T(8,128)S(1)}, u32[]{:S(2)}) copy-start(f32[512,512,8]{1,0,2:T(8,128)S(1)} %get-tuple-element.55) | copy-start | bytes 25165828
  128.2 16.9 %all-to-all-start.4 = ((bf16[4,128,256]{1,2,0:T(8,128)(2,1)}), bf16[4,128,256]{1,2,0:T(8,128)(2,1)S(1)}, u32[]{:S(2)}, u32[]{:S(2)}) async-start(bf16[4,128,256]{1,2,0:T(8,128)(2,1)} %pad_maximum_fusion.1), calls=%async_computation.4 | async-start | bytes 524288 | tf_op jit(solution)/shard_map/all_to_all | solution.py:162
  145.1 28.4 %all-to-all-start.3 = ((bf16[4,128,1024]{1,2,0:T(8,128)(2,1)}), bf16[4,128,1024]{1,2,0:T(8,128)(2,1)S(1)}, u32[]{:S(2)}, u32[]{:S(2)}) async-start(bf16[4,128,1024]{1,2,0:T(8,128)(2,1)} %copy.70), calls=%async_computation.3 | async-start | bytes 2097152 | tf_op jit(solution)/shard_map/all_to_all | solution.py:158
where the time goes:
time: 176 us; the launch traced here: 175 us
  waiting for transfers between devices  64.2 us (36%)
  blocking collectives  26.7 us (15%)
  starting transfers between devices  26.2 us (15%)
  local copies, waits for them, and re-layouts  24.3 us (14%)
  matrix products  17.5 us (10%)
  other arithmetic  14.9 us (8%)
    all_gather x1, blocking collectives, body(): full_seg = lax.all_gather(segment_labels, 'sp', axis=1, tiled=True)[0]  26.7 us
    all_to_all x1, waiting for transfers between devices, body(): lax.all_to_all(outgoing.reshape(dp_size, capacity, row_width), 'dp', spli...  23.5 us
    all_to_all x1, waiting for transfers between devices, body(): lax.all_to_all(query_back, 'sp', split_axis=0, concat_axis=2, tiled=True)  22.2 us
    all_to_all x1, waiting for transfers between devices, body(): lax.all_to_all(weighted_result.reshape(token_rows, sequence_split_size, p...  17.1 us
    dot_general x1, matrix products, body(): jnp.einsum('hbk,kd->bhd', score_grads, key_part, preferred_element_type=j...  7.8 us
    all_to_all x1, starting transfers between devices, body(): lax.all_to_all(partial_value.astype(jnp.bfloat16), 'sp', split_axis=0, co...  7.66 us
    all_to_all x1, starting transfers between devices, body(): lax.all_to_all(weighted_result.reshape(token_rows, sequence_split_size, p...  5.68 us
    all_to_all x1, starting transfers between devices, body(): lax.all_to_all(query_back, 'sp', split_axis=0, concat_axis=2, tiled=True)  5.09 us
  transfers between devices with their start and end apart: 5, of which 4 were waited for; matrix products, arithmetic and copies ran while one was open for 17% of the time, Pallas kernels for 0%

commit v1 on v0

--- a/solution.py
+++ b/solution.py
@@ -4,6 +4,7 @@
 import numpy as np
 from jax import lax
 from jax.sharding import PartitionSpec as P
+from jax.lax import all_to_all, psum
 
 QUERY_HEADS = 32
 KEY_VALUE_HEADS = 4
@@ -155,7 +156,11 @@
     query_back = jnp.concatenate(query_parts, axis=0).reshape(
         sequence_split_size, token_rows, per_dev * HEAD_SIZE
     )
-    query_gradient = lax.all_to_all(query_back, "sp", split_axis=0, concat_axis=2, tiled=True)
+    report_the_scenes = lambda ax_name, my_tile: jnp.concatenate(
+        all_to_all(jnp.stack(jnp.split(my_tile, psum(1, ax_name), axis=0), axis=0), ax_name, 0, 0),
+        axis=2,
+    )
+    query_gradient = report_the_scenes("sp", query_back)
     partial_value = jnp.concatenate([key_total, value_total], axis=1).reshape(
         sequence_split_size, token_rows, 2 * HEAD_SIZE
     )

time: 176 us -> 175 us (level)
  waiting for transfers between devices: 64.2 us -> 68.3 us
  local copies, waits for them, and re-layouts: 24.3 us -> 21.1 us
  matrix products: 17.5 us -> 15.1 us
  other arithmetic: 14.9 us -> 16.8 us
    all_to_all x1, waiting for transfers between devices: 0.01 us -> 5.39 us  [body(): lax.all_to_all(partial_value.astype(jnp.bfloat16), 'sp', split_axis=0, co...]
    dot_general x1, matrix products: 7.8 us -> 4.3 us  [body(): jnp.einsum('hbk,kd->bhd', score_grads, key_part, preferred_element_type=j...]
    slice x2, local copies, waits for them, and re-layouts: 2.6 us -> 0.67 us  [body(): local_rows[:, :per_dev * HEAD_SIZE].reshape(seq_len, per_dev, HEAD_SIZE)]
    unnamed x14 -> x15, local copies, waits for them, and re-layouts: 3.9 us -> 2.5 us
  transfers between devices with their start and end apart: 5 -> 5, of which waited for: 4 -> 5; matrix products, arithmetic and copies ran while one was open for 17% -> 13% of each run, Pallas kernels for 0% -> 0%
where the time goes in v1:
time: 175 us; the launch traced here: 174 us
  waiting for transfers between devices  68.3 us (39%)
  blocking collectives  26.7 us (15%)
  starting transfers between devices  25.3 us (14%)
  local copies, waits for them, and re-layouts  21.1 us (12%)
  other arithmetic  16.8 us (10%)
  matrix products  15.1 us (9%)
    all_gather x1, blocking collectives, body(): full_seg = lax.all_gather(segment_labels, 'sp', axis=1, tiled=True)[0]  26.7 us
    all_to_all x1, waiting for transfers between devices, body(): lax.all_to_all(outgoing.reshape(dp_size, capacity, row_width), 'dp', spli...  23.5 us
    all_to_all x1, waiting for transfers between devices, body(): all_to_all(jnp.stack(jnp.split(my_tile, psum(1, ax_name), axis=0), axis=0...  21.6 us
    all_to_all x1, waiting for transfers between devices, body(): lax.all_to_all(weighted_result.reshape(token_rows, sequence_split_size, p...  17.1 us
    all_to_all x1, starting transfers between devices, body(): lax.all_to_all(partial_value.astype(jnp.bfloat16), 'sp', split_axis=0, co...  8.34 us
    all_to_all x1, starting transfers between devices, body(): lax.all_to_all(weighted_result.reshape(token_rows, sequence_split_size, p...  5.68 us
    all_to_all x1, waiting for transfers between devices, body(): lax.all_to_all(partial_value.astype(jnp.bfloat16), 'sp', split_axis=0, co...  5.39 us
    scatter x1, local copies, waits for them, and re-layouts, body(): outgoing = jnp.zeros((dp_size * capacity, row_width), rollout_rows.dtype)...  5.01 us
  transfers between devices with their start and end apart: 5, of which 5 were waited for; matrix products, arithmetic and copies ran while one was open for 13% of the time, Pallas kernels for 0%

profile of v1, /device:TPU:0, one launch (start us, length us, event | category | flops | bytes accessed | tf_op | source)
XLA Modules:
  0.0 174.3 jit_solution(14704799677196582048)
XLA Ops:
  0.7 0.7 fusion.36
  1.5 0.2 reduce_window_sum.18
  1.6 0.2 select_reduce_fusion.1
  1.8 0.7 fusion.32
  2.5 5.0 %scatter_custom_fusion = bf16[256,5120]{1,0:T(8,128)(2,1)} fusion(s32[128]{0:T(128)S(1)} %fusion.32, bf16[128,5120]{1,0:T(8,128)(2,1)} %param.16, bf16[]{:T(256)} %constant.129.clone.1), kind=kCustom, calls=%fused_computation.24 | custom fusion | bytes 2621952 | tf_op jit(solution)/shard_map/scatter | solution.py:63
  7.5 4.2 %all-to-all-start = ((bf16[4,64,5120]{2,1,0:T(8,128)(2,1)}), bf16[4,64,5120]{2,1,0:T(8,128)(2,1)S(1)}, u32[]{:S(2)}, u32[]{:S(2)}) async-start(bf16[4,64,5120]{2,1,0:T(8,128)(2,1)} %bitcast.131), calls=%async_computation | async-start | bytes 5242880 | tf_op jit(solution)/shard_map/all_to_all | solution.py:65
  11.8 3.7 %reshape.292 = f32[128,4,1024]{2,1,0:T(4,128)} reshape(bf16[1,128,4096]{2,1,0:T(8,128)(2,1)} %param.19) | data formatting | bytes 3145728 | tf_op jit(solution)/shard_map/convert_element_type | solution.py:100
  15.5 0.1 convert_reduce_fusion.1
  15.6 0.1 select_reduce_fusion.3
  15.9 3.7 %fusion.11 = bf16[128,4,1024]{2,0,1:T(8,128)(2,1)} fusion(f32[128,4,1024]{2,1,0:T(4,128)} %reshape.292, f32[128]{0:T(128)S(1)} %select_reduce_fusion.2), kind=kLoop, calls=%fused_computation.20 | loop fusion | flops 1048576 | bytes 3146240 | tf_op jit(solution)/shard_map/convert_element_type | solution.py:100
  19.6 23.5 %all-to-all-done = bf16[4,64,5120]{2,1,0:T(8,128)(2,1)S(1)} async-done(((bf16[4,64,5120]{2,1,0:T(8,128)(2,1)}), bf16[4,64,5120]{2,1,0:T(8,128)(2,1)S(1)}, u32[]{:S(2)}, u32[]{:S(2)}) %all-to-all-start) | async-done | bytes 2621472 | tf_op jit(solution)/shard_map/all_to_all | solution.py:65
  43.1 5.7 %all-to-all-start.2 = ((bf16[128,4,1024]{2,0,1:T(8,128)(2,1)}), bf16[128,4,1024]{2,0,1:T(8,128)(2,1)}, u32[]{:S(2)}, u32[]{:S(2)}) async-start(bf16[128,4,1024]{2,0,1:T(8,128)(2,1)} %fusion.11), calls=%async_computation.2 | async-start | bytes 2097152 | tf_op jit(solution)/shard_map/all_to_all | solution.py:101
  48.8 0.9 fusion.31
  49.6 0.2 reduce-window.7
  49.9 0.2 select_reduce_fusion
  50.1 2.4 %gather_fusion = bf16[128,5120]{1,0:T(8,128)(2,1)} fusion(bf16[256,5120]{1,0:T(8,128)(2,1)S(1)} %bitcast.129, s32[1024]{0:T(1024)S(1)} %pad_clamp_fusion.1), kind=kCustom, calls=%fused_computation | custom fusion | bytes 2621952 | tf_op jit(solution)/shard_map/gather | solution.py:79
  52.5 1.0 slice.57
  53.5 1.3 slice.56
  54.9 0.2 reshape.285
  55.1 0.6 gather_fusion.1
  55.7 0.2 copy.47
  55.9 0.1 copy.49
  56.0 1.2 pad_maximum_fusion
  57.2 17.1 %all-to-all-done.2 = bf16[128,4,1024]{2,0,1:T(8,128)(2,1)} async-done(((bf16[128,4,1024]{2,0,1:T(8,128)(2,1)}), bf16[128,4,1024]{2,0,1:T(8,128)(2,1)}, u32[]{:S(2)}, u32[]{:S(2)}) %all-to-all-start.2) | async-done | bytes 1048608 | tf_op jit(solution)/shard_map/all_to_all | solution.py:101
  74.3 3.5 %all-to-all-start.1 = ((bf16[128,4,1280]{2,0,1:T(8,128)(2,1)}), bf16[128,4,1280]{2,0,1:T(8,128)(2,1)S(1)}, u32[]{:S(2)}, u32[]{:S(2)}) async-start(bf16[128,4,1280]{2,0,1:T(8,128)(2,1)} %pad_maximum_fusion), calls=%async_computation.1 | async-start | bytes 2621440 | tf_op jit(solution)/shard_map/all_to_all | solution.py:82
  77.9 26.7 %all_gather.3 = s32[1,512]{1,0:T(1,128)S(1)} all-gather(s32[1,128]{1,0:T(1,128)S(1)} %copy-done.4), channel_id=1, replica_groups=mesh['grp'=2,'dp'=4,'sp'=4] {'sp'}, dimensions={1}, use_global_device_ids=true | all-gather | bytes 2560 | tf_op jit(solution)/shard_map/all_gather | solution.py:90
  104.6 1.0 fusion.30
  105.6 2.5 %copy.69 = bf16[64,8,8,128]{3,2,1,0:T(8,128)(2,1)} copy(bf16[64,8,8,128]{3,1,2,0:T(8,128)(2,1)} %bitcast.59) | data formatting | bytes 2097152
  108.1 0.7 all-to-all-done.1
  108.8 0.1 slice.59
  108.9 0.5 copy.50
  109.5 2.6 %fusion.4 = (f32[8,512]{1,0:T(8,128)S(1)}, f32[512,512,8]{1,0,2:T(8,128)S(1)}) fusion(pred[512,512]{0,1:T(8,128)(4,1)} %get-tuple-element.51, bf16[512,8,128]{0,2,1:T(8,128)(2,1)S(1)} %bitcast.136, bf16[512,1280]{1,0:T(8,128)(2,1)S(1)} %bitcast.133), kind=kOutput, calls=%fused_computation.13 | convolution fusion | flops 543158272 | bytes 9846784 | tf_op jit(solution)/shard_map/bhd,kd->hbk/dot_general | solution.py:125
  112.1 1.8 %fusion.6 = f32[8,512]{1,0:T(8,128)S(1)} fusion(f32[512,512,8]{1,0,2:T(8,128)S(1)} %get-tuple-element.53, f32[8,512]{1,0:T(8,128)S(1)} %get-tuple-element.52, pred[512,512]{0,1:T(8,128)(4,1)S(1)} %copy-done.1), kind=kLoop, calls=%fused_computation.15 | loop fusion | flops 8384512 | bytes 8683520 | tf_op jit(solution)/shard_map/reduce_sum | solution.py:134
  113.8 3.0 %fusion = (f32[8,512]{1,0:T(8,128)S(1)}, f32[512,512,8]{1,0,2:T(8,128)S(1)}) fusion(f32[8,512]{1,0:T(8,128)S(1)} %fusion.6, f32[8,512]{1,0:T(8,128)S(1)} %get-tuple-element.52, f32[512,512,8]{1,0,2:T(8,128)S(1)} %get-tuple-element.53, pred[512,512]{0,1:T(8,128)(4,1)S(1)} %copy-done.1, bf16[512,8,128]{2,1,0:T(8,128)(2,1)S(1)} %bitcast.141, ...), kind=kOutput, calls=%fused_computation.5 | convolution fusion | flops 549449728 | bytes 18268160 | tf_op jit(solution)/shard_map/bhd,kd->hbk/dot_general | solution.py:135
  116.8 4.3 %fusion.15 = bf16[512,8,128]{0,2,1:T(8,128)(2,1)} fusion(f32[512,512,8]{1,0,2:T(8,128)S(1)} %get-tuple-element.55, f32[8,512]{1,0:T(8,128)S(1)} %get-tuple-element.54, f32[512,512,8]{1,0,2:T(8,128)S(1)} %get-tuple-element.53, f32[8,512]{1,0:T(8,128)S(1)} %fusion.6, f32[8,512]{1,0:T(8,128)S(1)} %get-tuple-element.52, pred[512,512]{0,1:T(8,128)(4,1)S(1)} %copy-done.1, ...), kind=kOutput, calls=%fused_computation.22 | convolution fusion | flops 554172416 | bytes 18268160 | tf_op jit(solution)/shard_map/hbk,kd->bhd/dot_general | solution.py:141
  121.2 4.6 %multiply_convert_fusion = (bf16[512,512,8]{1,0,2:T(8,128)(2,1)}, bf16[512,512,8]{1,0,2:T(8,128)(2,1)S(1)}) fusion(f32[512,512,8]{1,0,2:T(8,128)S(1)} %get-tuple-element.55, f32[512,8]{0,1:T(8,128)S(1)} %bitcast.154, f32[512,8]{0,1:T(8,128)S(1)} %bitcast.152, f32[512,8]{0,1:T(8,128)S(1)} %bitcast.151, f32[512,512,8]{1,0,2:T(8,128)S(1)} %get-tuple-element.53, ...), kind=kLoop, calls=%fused_computation.10 | loop fusion | flops 18874368 | bytes 25477120 | tf_op jit(solution)/shard_map/convert_element_type | solution.py:139
  125.7 3.7 %fusion.22 = bf16[4,128,128]{1,2,0:T(8,128)(2,1)S(1)} fusion(bf16[4,128,512,8]{2,1,0,3:T(8,128)(2,1)} %bitcast.143, bf16[512,8,128,1]{0,2,3,1:T(8,128)(2,1)S(1)} %bitcast.137), kind=kOutput, calls=%fused_computation.29 | convolution fusion | flops 536936448 | bytes 5373952 | tf_op jit(solution)/shard_map/hbk,bhd->kd/dot_general | solution.py:146
  129.4 1.5 fusion.23
  131.0 0.7 pad_maximum_fusion.2
  131.7 8.3 %all-to-all-start.4 = ((bf16[4,128,256]{1,2,0:T(8,128)(2,1)}), bf16[4,128,256]{1,2,0:T(8,128)(2,1)S(1)}, u32[]{:S(2)}, u32[]{:S(2)}) async-start(bf16[4,128,256]{1,2,0:T(8,128)(2,1)} %pad_maximum_fusion.2), calls=%async_computation.4 | async-start | bytes 524288 | tf_op jit(solution)/shard_map/all_to_all | solution.py:167
  140.0 0.3 fusion.38
  140.3 1.1 pad_maximum_fusion.1
  141.4 5.4 %all-to-all-done.4 = bf16[4,128,256]{1,2,0:T(8,128)(2,1)S(1)} async-done(((bf16[4,128,256]{1,2,0:T(8,128)(2,1)}), bf16[4,128,256]{1,2,0:T(8,128)(2,1)S(1)}, u32[]{:S(2)}, u32[]{:S(2)}) %all-to-all-start.4) | async-done | bytes 262176 | tf_op jit(solution)/shard_map/all_to_all | solution.py:167
  146.8 3.5 %all-to-all-start.3 = ((bf16[4,1,128,1024]{2,3,1,0:T(8,128)(2,1)}), bf16[4,1,128,1024]{2,3,1,0:T(8,128)(2,1)S(1)}, u32[]{:S(2)}, u32[]{:S(2)}) async-start(bf16[4,1,128,1024]{2,3,1,0:T(8,128)(2,1)} %pad_maximum_fusion.1), calls=%async_computation.3 | async-start | bytes 2097152 | tf_op jit(solution)/shard_map/all_to_all | solution.py:160
  150.3 0.2 copy.58
  150.5 0.9 convert_element_type.78
  151.4 21.6 %all-to-all-done.3 = bf16[4,1,128,1024]{2,3,1,0:T(8,128)(2,1)S(1)} async-done(((bf16[4,1,128,1024]{2,3,1,0:T(8,128)(2,1)}), bf16[4,1,128,1024]{2,3,1,0:T(8,128)(2,1)S(1)}, u32[]{:S(2)}, u32[]{:S(2)}) %all-to-all-start.3) | async-done | bytes 1048608 | tf_op jit(solution)/shard_map/all_to_all | solution.py:160
  173.0 1.3 copy.65
  (28 shorter events, 0.5 us)
Async XLA Ops:
  0.6 14.8 %copy-start.6 = (s32[16]{0:T(128)S(1)}, s32[16]{0:T(128)}, u32[]{:S(2)}) copy-start(s32[16]{0:T(128)} %param.20) | copy-start | bytes 196
  0.6 14.8 %copy-start.5 = (s32[16]{0:T(128)S(1)}, s32[16]{0:T(128)}, u32[]{:S(2)}) copy-start(s32[16]{0:T(128)} %param.21) | copy-start | bytes 196
  0.7 15.1 %copy-start.4 = (s32[1,128]{1,0:T(1,128)S(1)}, s32[1,128]{1,0:T(1,128)}, u32[]{:S(2)}) copy-start(s32[1,128]{1,0:T(1,128)} %param.18) | copy-start | bytes 1540
  7.5 35.6 %all-to-all-start = ((bf16[4,64,5120]{2,1,0:T(8,128)(2,1)}), bf16[4,64,5120]{2,1,0:T(8,128)(2,1)S(1)}, u32[]{:S(2)}, u32[]{:S(2)}) async-start(bf16[4,64,5120]{2,1,0:T(8,128)(2,1)} %bitcast.131), calls=%async_computation | async-start | bytes 5242880 | tf_op jit(solution)/shard_map/all_to_all | solution.py:65
  43.1 31.2 %all-to-all-start.2 = ((bf16[128,4,1024]{2,0,1:T(8,128)(2,1)}), bf16[128,4,1024]{2,0,1:T(8,128)(2,1)}, u32[]{:S(2)}, u32[]{:S(2)}) async-start(bf16[128,4,1024]{2,0,1:T(8,128)(2,1)} %fusion.11), calls=%async_computation.2 | async-start | bytes 2097152 | tf_op jit(solution)/shard_map/all_to_all | solution.py:101
  74.3 34.4 %all-to-all-start.1 = ((bf16[128,4,1280]{2,0,1:T(8,128)(2,1)}), bf16[128,4,1280]{2,0,1:T(8,128)(2,1)S(1)}, u32[]{:S(2)}, u32[]{:S(2)}) async-start(bf16[128,4,1280]{2,0,1:T(8,128)(2,1)} %pad_maximum_fusion), calls=%async_computation.1 | async-start | bytes 2621440 | tf_op jit(solution)/shard_map/all_to_all | solution.py:82
  109.4 2.6 %copy-start.1 = (pred[512,512]{0,1:T(8,128)(4,1)S(1)}, pred[512,512]{0,1:T(8,128)(4,1)}, u32[]{:S(2)}) copy-start(pred[512,512]{0,1:T(8,128)(4,1)} %get-tuple-element.51) | copy-start | bytes 786436
  109.5 4.4 %copy-start = (bf16[64,8,8,128]{3,2,1,0:T(8,128)(2,1)S(1)}, bf16[64,8,8,128]{3,2,1,0:T(8,128)(2,1)}, u32[]{:S(2)}) copy-start(bf16[64,8,8,128]{3,2,1,0:T(8,128)(2,1)} %copy.69) | copy-start | bytes 3145732
  116.8 4.3 %copy-start.2 = (pred[512,512]{1,0:T(8,128)(4,1)S(1)}, pred[512,512]{1,0:T(8,128)(4,1)}, u32[]{:S(2)}) copy-start(pred[512,512]{1,0:T(8,128)(4,1)} %get-tuple-element.50) | copy-start | bytes 786436
  125.7 14.3 %copy-start.3 = (bf16[512,8,128]{0,2,1:T(8,128)(2,1)S(1)}, bf16[512,8,128]{0,2,1:T(8,128)(2,1)}, u32[]{:S(2)}) copy-start(bf16[512,8,128]{0,2,1:T(8,128)(2,1)} %fusion.15) | copy-start | bytes 3145732
  131.7 15.1 %all-to-all-start.4 = ((bf16[4,128,256]{1,2,0:T(8,128)(2,1)}), bf16[4,128,256]{1,2,0:T(8,128)(2,1)S(1)}, u32[]{:S(2)}, u32[]{:S(2)}) async-start(bf16[4,128,256]{1,2,0:T(8,128)(2,1)} %pad_maximum_fusion.2), calls=%async_computation.4 | async-start | bytes 524288 | tf_op jit(solution)/shard_map/all_to_all | solution.py:167
  146.8 26.2 %all-to-all-start.3 = ((bf16[4,1,128,1024]{2,3,1,0:T(8,128)(2,1)}), bf16[4,1,128,1024]{2,3,1,0:T(8,128)(2,1)S(1)}, u32[]{:S(2)}, u32[]{:S(2)}) async-start(bf16[4,1,128,1024]{2,3,1,0:T(8,128)(2,1)} %pad_maximum_fusion.1), calls=%async_computation.3 | async-start | bytes 2097152 | tf_op jit(solution)/shard_map/all_to_all | solution.py:160
